TPU v7x, 256 devices: a whole 4x4x8 slice. The times are simulated.
256 devices in a mesh: expert: 16 (over y_hi, z), mp: 8 (over y_lo, x), batch: 2 (over core).
Axes of the slice: x: 4, y: 4 (y_hi: 2, y_lo: 2; y = y_hi * 2 + y_lo), z: 8, core: 2. Of those that a mesh axis runs over, the one named last changes fastest.
Arguments:
- tokens: bfloat16 [2, 2048, 2880], P('batch', 'expert', 'mp'), may hold values from -6 to 6
- segments: int32 [2, 2048], P('batch'), may hold values from 0 to 63, never falling along the last dimension, each value on 1 to 1024 neighbouring positions
- attn_gain: float32 [2880], replicated, may hold values from 0.6 to 9
- w_query: bfloat16 [2880, 4096], P('expert', 'mp'), may hold values from -0.109375 to 0.109375
- key_weight: bfloat16 [2880, 512], P('expert', 'mp'), may hold values from -0.109375 to 0.109375
- value_weight: bfloat16 [2880, 512], P('expert', 'mp'), may hold values from -0.109375 to 0.109375
- w_out: bfloat16 [4096, 2880], P('mp', 'expert'), may hold values from -0.09375 to 0.09375
- sink_head_logit: float32 [64], P('mp'), may hold values from -4 to 4
- moe_gain: float32 [2880], replicated, may hold values from 0.5 to 1.5
- expert_in: bfloat16 [16, 2, 2880, 2880], P('expert', None, None, 'mp'), may hold values from -0.3125 to 0.3125
- expert_down: bfloat16 [16, 2880, 2880], P('expert', 'mp'), may hold values from -0.01953125 to 0.01953125
- routes: int32 [2, 2048, 4], P('batch', 'expert'), may hold values from 0 to 15, all different within a row; in each aligned block of 128 rows (0 to 127, 128 to 255, ..., all dimensions but the last counted through in order) at most 48 rows name the same one
- route_weights: float32 [2, 2048, 4], P('batch', 'expert'), may hold values from 0.1 to 1
Outputs:
- hidden: bfloat16 [2, 2048, 2880], P('batch', 'expert', 'mp')
- key_cache: bfloat16 [2, 2048, 512], P('batch', 'expert', 'mp')
- value_cache: bfloat16 [2, 2048, 512], P('batch', 'expert', 'mp')
Inputs may be any that keep to these rules, and one draw needn't show every extreme that they name: Within each aligned block of 128 tokens of a micro-batch (the tokens of one index of expert), no expert is named by more than 48 routes; a token's routes name different experts. `segments`: segment numbers never fall along a micro-batch; one segment holds at most 1024 tokens.
All inputs are finite; a program needn't handle non-finite values.
Results may differ from a plain program's by a relative error of at most 0.024.
The roundings to bfloat16 on the way count: a program that leaves them out, or rounds other values in their place, can miss the bound.
Values may be sent and summed in bfloat16 or wider, within the bound.
No kernel may reach another device: no remote copies, remote signals or barrier semaphores. Data moves between devices by JAX's collectives and lax.ppermute only.
A program may use at most 64 MiB of HBM per device.

v0:
```python
import math
import jax
import jax.numpy as jnp
from jax import lax
from jax.sharding import PartitionSpec as P

HEAD_SIZE = 64
eps = 1e-05
rope_base = 150000.0
clamp_limit = 7.0
glu_alpha = 1.702


def rms_norm(row_block, gain):
    values = row_block.astype(jnp.float32)
    inv_scale = lax.rsqrt(jnp.mean(values * values, axis=-1, keepdims=True) + eps)
    return (values * inv_scale * gain).astype(jnp.bfloat16)


def apply_rotary(values, token_positions):
    half_dim = values.shape[-1] // 2
    inv_freq = jnp.power(
        rope_base, -2.0 * jnp.arange(half_dim, dtype=jnp.float32) / values.shape[-1]
    )
    rot_angle = token_positions.astype(jnp.float32)[:, None] * inv_freq[None, :]
    cosine = jnp.cos(rot_angle)[:, None, :]
    sine_val = jnp.sin(rot_angle)[:, None, :]
    first_half = values[..., :half_dim]
    second_half = values[..., half_dim:]
    return jnp.concatenate(
        [
            first_half * cosine - second_half * sine_val,
            second_half * cosine + first_half * sine_val,
        ],
        axis=-1,
    )


def gather_by_exchange(block, axis_name):
    count = lax.axis_size(axis_name)
    spread = jnp.broadcast_to(block[None], (count,) + block.shape)
    got = lax.all_to_all(spread, axis_name, split_axis=0, concat_axis=0, tiled=True)
    return got.reshape((count * block.shape[0],) + block.shape[1:])


def expert_rows(row_block, w_in, w_down):
    gate_val = jnp.dot(row_block, w_in[0], preferred_element_type=jnp.float32)
    up_val = jnp.dot(row_block, w_in[1], preferred_element_type=jnp.float32)
    gate_val = jnp.minimum(gate_val, clamp_limit)
    up_val = jnp.clip(up_val, -clamp_limit, clamp_limit)
    activated = ((up_val + 1.0) * gate_val * jax.nn.sigmoid(glu_alpha * gate_val)).astype(
        jnp.bfloat16
    )
    return jnp.dot(activated, w_down, preferred_element_type=jnp.float32)


def shards(
    tokens,
    segments,
    attn_gain,
    w_query,
    key_weight,
    value_weight,
    w_out,
    sink_head_logit,
    moe_gain,
    expert_in,
    expert_down,
    routes,
    route_weights,
):
    local_rows = tokens[0]
    tok_count = local_rows.shape[0]
    expert_devs = lax.axis_size("expert")
    row_start = lax.axis_index("expert") * tok_count
    mp_devs = lax.axis_size("mp")
    whole_rows = gather_by_exchange(local_rows.T, "mp").reshape(-1, tok_count).T
    input_normalised = rms_norm(whole_rows, attn_gain)
    query_cols = w_query.shape[1]
    kv_cols = key_weight.shape[1]
    shard_rows = w_query.shape[0]
    padded_rows = -(-shard_rows // 8) * 8
    big_weights = lax.all_gather(
        jnp.pad(
            jnp.concatenate([w_query, w_out.T], axis=1), ((0, padded_rows - shard_rows), (0, 0))
        ),
        "expert",
        axis=0,
    )
    query_weight = big_weights[:, :, :query_cols].reshape(expert_devs * padded_rows, query_cols)
    out_weight_t = big_weights[:, :, query_cols:]
    kv_weight = gather_by_exchange(jnp.concatenate([key_weight, value_weight], axis=1), "expert")
    normed_padded = jnp.pad(
        input_normalised.reshape(tok_count, expert_devs, shard_rows),
        ((0, 0), (0, 0), (0, padded_rows - shard_rows)),
    ).reshape(tok_count, expert_devs * padded_rows)
    query_raw = jnp.dot(normed_padded, query_weight, preferred_element_type=jnp.float32)
    kv_raw = jnp.dot(input_normalised, kv_weight, preferred_element_type=jnp.float32)
    key_raw = kv_raw[:, :kv_cols]
    value_raw = kv_raw[:, kv_cols:]
    token_positions = row_start + jnp.arange(tok_count, dtype=jnp.int32)
    query_by_head = query_cols // HEAD_SIZE
    kv_heads = kv_cols // HEAD_SIZE
    heads_per_group = query_by_head // kv_heads
    query_matrix = apply_rotary(
        query_raw.reshape(tok_count, query_by_head, HEAD_SIZE), token_positions
    ).astype(jnp.bfloat16)
    key_rotary = (
        apply_rotary(key_raw.reshape(tok_count, kv_heads, HEAD_SIZE), token_positions)
        .astype(jnp.bfloat16)
        .reshape(tok_count, kv_cols)
    )
    value_fresh = value_raw.astype(jnp.bfloat16)
    kv_all = gather_by_exchange(jnp.concatenate([key_rotary, value_fresh], axis=1), "expert")
    keys_all = kv_all[:, :kv_cols]
    values_all = kv_all[:, kv_cols:]
    seq_len = keys_all.shape[0]
    seg_all = segments[0]
    seg_local = lax.dynamic_slice_in_dim(seg_all, row_start, tok_count)
    row_total = heads_per_group * tok_count
    query_rows = (
        query_matrix.reshape(tok_count, kv_heads, heads_per_group, HEAD_SIZE)
        .transpose(1, 2, 0, 3)
        .reshape(kv_heads, row_total, HEAD_SIZE)
    )
    key_by_head = keys_all.reshape(seq_len, kv_heads, HEAD_SIZE).transpose(1, 0, 2)
    value_by_head = values_all.reshape(seq_len, kv_heads, HEAD_SIZE).transpose(1, 0, 2)
    row_pos = jnp.tile(token_positions, heads_per_group)
    row_seg = jnp.tile(seg_local, heads_per_group)
    sink_rows = jnp.repeat(sink_head_logit.reshape(kv_heads, heads_per_group), tok_count, axis=1)
    key_block = math.gcd(seq_len, 2048)
    block_count = seq_len // key_block
    score_scale = HEAD_SIZE ** (-0.5)

    def block_scores(index):
        key_first = index * key_block
        key_part = lax.dynamic_slice_in_dim(key_by_head, key_first, key_block, 1)
        scores = (
            jnp.einsum("hrd,hkd->hrk", query_rows, key_part, preferred_element_type=jnp.float32)
            * score_scale
        )
        key_pos = key_first + jnp.arange(key_block, dtype=jnp.int32)
        key_seg = lax.dynamic_slice_in_dim(seg_all, key_first, key_block, 0)
        allowed = (key_pos[None, :] <= row_pos[:, None]) & (key_seg[None, :] == row_seg[:, None])
        return jnp.where(allowed[None], scores, -jnp.inf)

    def max_step(index, running):
        return jnp.maximum(running, jnp.max(block_scores(index), axis=-1))

    row_max = lax.fori_loop(0, block_count, max_step, sink_rows)

    def sum_step(index, carried):
        weighted, denom = carried
        probs = jnp.exp(block_scores(index) - row_max[..., None]).astype(jnp.bfloat16)
        value_part = lax.dynamic_slice_in_dim(value_by_head, index * key_block, key_block, 1)
        weighted = weighted + jnp.einsum(
            "hrk,hkd->hrd", probs, value_part, preferred_element_type=jnp.float32
        )
        denom = denom + jnp.sum(probs, axis=-1, dtype=jnp.float32)
        return (weighted, denom)

    init_pair = (
        jnp.zeros((kv_heads, row_total, HEAD_SIZE), jnp.float32),
        jnp.zeros((kv_heads, row_total), jnp.float32),
    )
    weighted, denom = lax.fori_loop(0, block_count, sum_step, init_pair)
    denom = denom + jnp.exp(sink_rows - row_max)
    mixed = (weighted / denom[..., None]).astype(jnp.bfloat16)
    mixed = (
        mixed.reshape(kv_heads, heads_per_group, tok_count, HEAD_SIZE)
        .transpose(2, 0, 1, 3)
        .reshape(tok_count, query_cols)
    )
    out_terms_t = jnp.einsum(
        "efc,tc->eft", out_weight_t, mixed, preferred_element_type=jnp.float32
    )[:, :shard_rows]
    model_width = out_terms_t.shape[0] * out_terms_t.shape[1]
    out_pieces = out_terms_t.astype(jnp.bfloat16).reshape(
        mp_devs, model_width // mp_devs, tok_count
    )
    out_got = lax.all_to_all(out_pieces, "mp", split_axis=0, concat_axis=0, tiled=True)
    attn_part = jnp.sum(out_got.astype(jnp.float32), axis=0).T
    first_out = (local_rows.astype(jnp.float32) + attn_part).astype(jnp.bfloat16)
    top_count = routes.shape[2]
    local_experts = expert_in.shape[0]
    expert_count = local_experts * expert_devs
    capacity = 3 * tok_count * top_count // (2 * expert_count)
    chosen = routes[0].reshape(tok_count * top_count)
    onehot = (chosen[:, None] == jnp.arange(expert_count, dtype=jnp.int32)[None, :]).astype(
        jnp.int32
    )
    ranks = jnp.sum((jnp.cumsum(onehot, axis=0) - onehot) * onehot, axis=1)
    target = chosen * capacity + ranks
    source_row = (
        jnp.full((expert_count * capacity,), tok_count, jnp.int32)
        .at[target]
        .set(jnp.arange(tok_count * top_count, dtype=jnp.int32) // top_count)
    )
    padded = jnp.concatenate([first_out, jnp.zeros((1, first_out.shape[1]), jnp.bfloat16)], axis=0)
    pick = (source_row[:, None] == jnp.arange(tok_count + 1, dtype=jnp.int32)[None, :]).astype(
        jnp.bfloat16
    )
    outgoing = (
        jnp.dot(pick, padded, preferred_element_type=jnp.float32)
        .astype(jnp.bfloat16)
        .reshape(expert_count, capacity, padded.shape[1])
    )
    arrived = lax.all_to_all(outgoing, "expert", split_axis=0, concat_axis=0, tiled=True)
    arrived_rows = arrived.reshape(expert_count * capacity, arrived.shape[2])
    inputs = rms_norm(lax.all_gather(arrived_rows, "mp", axis=1, tiled=True), moe_gain)
    w_in = expert_in[0]
    hidden_cols = w_in.shape[2]
    inputs = lax.optimization_barrier(inputs)
    gate_up = jnp.dot(
        inputs, jnp.concatenate([w_in[0], w_in[1]], axis=1), preferred_element_type=jnp.float32
    )
    gate_val = gate_up[:, :hidden_cols]
    up_val = gate_up[:, hidden_cols:]
    gate_val = jnp.minimum(gate_val, clamp_limit)
    up_val = jnp.clip(up_val, -clamp_limit, clamp_limit)
    activated = ((up_val + 1.0) * gate_val * jax.nn.sigmoid(glu_alpha * gate_val)).astype(
        jnp.bfloat16
    )
    activated = lax.optimization_barrier(activated)
    partials = jnp.einsum(
        "rh,hjf->jrf",
        activated,
        expert_down[0].reshape(expert_down.shape[1], mp_devs, -1),
        preferred_element_type=jnp.float32,
    )
    expert_out = lax.psum_scatter(
        partials.astype(jnp.bfloat16), "mp", scatter_dimension=0, tiled=True
    ).reshape(expert_count, capacity, -1)
    local_width = expert_out.shape[2]
    returned = lax.all_to_all(expert_out, "expert", split_axis=0, concat_axis=0, tiled=True)
    slot_pick = (
        target[:, None] == jnp.arange(expert_count * capacity, dtype=jnp.int32)[None, :]
    ).astype(jnp.bfloat16)
    picked = jnp.dot(
        slot_pick,
        returned.reshape(expert_count * capacity, local_width),
        preferred_element_type=jnp.float32,
    ).reshape(tok_count, top_count, local_width)
    moe_sum = jnp.sum(picked.astype(jnp.float32) * route_weights[0][..., None], axis=1)
    hidden = (first_out.astype(jnp.float32) + moe_sum).astype(jnp.bfloat16)
    return (hidden[None], key_rotary[None], value_fresh[None])


def solution(mesh):
    placed = (
        P("batch", "expert", "mp"),
        P("batch", None),
        P(),
        P("expert", "mp"),
        P("expert", "mp"),
        P("expert", "mp"),
        P("mp", "expert"),
        P("mp"),
        P(),
        P("expert", None, None, "mp"),
        P("expert", "mp", None),
        P("batch", "expert", None),
        P("batch", "expert", None),
    )
    return jax.shard_map(
        shards,
        mesh=mesh,
        in_specs=placed,
        out_specs=(
            P("batch", "expert", "mp"),
            P("batch", "expert", "mp"),
            P("batch", "expert", "mp"),
        ),
        check_vma=False,
    )
```

profile of v0, /device:TPU:1, one launch (start us, length us, event | category | flops | bytes accessed | tf_op | source)
XLA Modules:
  0.0 365.3 jit_solution(1830637323441085088)
XLA Ops:
  7.2 1.8 fusion.37
  9.1 1.9 broadcast_in_dim.29
  10.9 5.9 %all-to-all-start = ((bf16[8,360,128]{2,1,0:T(8,128)(2,1)}), bf16[8,360,128]{2,1,0:T(8,128)(2,1)S(1)}, u32[]{:S(2)}, u32[]{:S(2)}) async-start(bf16[8,360,128]{2,1,0:T(8,128)(2,1)} %broadcast_in_dim.29), calls=%async_computation | async-start | bytes 1474560 | tf_op jit(solution)/shard_map/all_to_all | solution.py:42
  19.3 1.2 reduce-window.6
  20.5 8.8 %all-to-all-done = bf16[8,360,128]{2,1,0:T(8,128)(2,1)S(1)} async-done(((bf16[8,360,128]{2,1,0:T(8,128)(2,1)}), bf16[8,360,128]{2,1,0:T(8,128)(2,1)S(1)}, u32[]{:S(2)}, u32[]{:S(2)}) %all-to-all-start) | async-done | bytes 737312 | tf_op jit(solution)/shard_map/all_to_all | solution.py:42
  30.2 10.6 %all-to-all-start.1 = ((bf16[16,180,128]{2,1,0:T(8,128)(2,1)}), bf16[16,180,128]{2,1,0:T(8,128)(2,1)S(1)}, u32[]{:S(2)}, u32[]{:S(2)}) async-start(bf16[16,180,128]{2,1,0:T(8,128)(2,1)} %broadcast_in_dim.30), calls=%async_computation.1 | async-start | bytes 1507328 | tf_op jit(solution)/shard_map/all_to_all | solution.py:42
  43.0 26.1 %all-to-all-done.1 = bf16[16,180,128]{2,1,0:T(8,128)(2,1)S(1)} async-done(((bf16[16,180,128]{2,1,0:T(8,128)(2,1)}), bf16[16,180,128]{2,1,0:T(8,128)(2,1)S(1)}, u32[]{:S(2)}, u32[]{:S(2)}) %all-to-all-start.1) | async-done | bytes 737312 | tf_op jit(solution)/shard_map/all_to_all | solution.py:42
  70.9 4.6 %all-to-all-start.2 = ((bf16[16,128,128]{2,1,0:T(8,128)(2,1)}), bf16[16,128,128]{2,1,0:T(8,128)(2,1)S(1)}, u32[]{:S(2)}, u32[]{:S(2)}) async-start(bf16[16,128,128]{2,1,0:T(8,128)(2,1)} %broadcast_in_dim.35), calls=%async_computation.2 | async-start | bytes 1048576 | tf_op jit(solution)/shard_map/all_to_all | solution.py:42
  77.6 66.0 %all-gather.6.cloned.1.call-done = bf16[2944,1024]{1,0:T(8,128)(2,1)} async-done(((bf16[184,1024]{1,0:T(8,128)(2,1)}), bf16[2944,1024]{1,0:T(8,128)(2,1)}) %all-gather.6.cloned.1.call-update) | async-done | bytes 6029328 | tf_op jit(solution)/shard_map/all_gather | solution.py:83
  143.6 3.7 %slice.73 = bf16[16,184,512]{2,1,0:T(8,128)(2,1)} slice(bf16[16,184,1024]{2,1,0:T(8,128)(2,1)} %bitcast.143), slice={[0:16], [0:184], [0:512]} | slice | bytes 6029312 | tf_op jit(solution)/shard_map/slice | solution.py:90
  147.3 3.3 copy.38
  150.7 2.1 fusion.67
  153.7 3.7 %fusion.4 = (f32[1024]{0:T(1024)S(1)}, f32[1024,2048]{1,0:T(8,128)S(1)}) fusion(s32[2048]{0:T(1024)} %bitcast.159, s32[1024]{0:T(1024)} %get-tuple-element.62, s32[1024]{0:T(1024)} %get-tuple-element.61, bf16[2048,128]{1,0:T(8,128)(2,1)S(1)} %bitcast.141, bf16[8,8,8,128]{3,2,1,0:T(8,128)(2,1)S(1)} %bitcast.152), kind=kOutput, calls=%fused_computation.11 | convolution fusion | flops 281017344 | bytes 9064448 | tf_op jit(solution)/shard_map/while/body/eval_jaxpr/hrd,hkd->hrk/dot_general | solution.py:139
  157.5 3.5 convert_reduce_fusion
  161.1 1.5 fusion.24
  164.7 4.0 %all-to-all-start.3 = ((bf16[8,360,128]{2,1,0:T(8,128)(2,1)}), bf16[8,360,128]{2,1,0:T(8,128)(2,1)S(1)}, u32[]{:S(2)}, u32[]{:S(2)}) async-start(bf16[8,360,128]{2,1,0:T(8,128)(2,1)} %reshape.428), calls=%async_computation.3 | async-start | bytes 1474560 | tf_op jit(solution)/shard_map/all_to_all | solution.py:181
  169.0 2.4 scatter_custom_fusion
  171.5 9.7 %all-to-all-done.3 = bf16[8,360,128]{2,1,0:T(8,128)(2,1)S(1)} async-done(((bf16[8,360,128]{2,1,0:T(8,128)(2,1)}), bf16[8,360,128]{2,1,0:T(8,128)(2,1)S(1)}, u32[]{:S(2)}, u32[]{:S(2)}) %all-to-all-start.3) | async-done | bytes 737312 | tf_op jit(solution)/shard_map/all_to_all | solution.py:181
  182.1 22.0 %all_to_all.30 = bf16[16,48,360]{2,1,0:T(8,128)(2,1)S(1)} all-to-all(bf16[16,48,360]{2,1,0:T(8,128)(2,1)S(1)} %bitcast.138), channel_id=1, replica_groups=mesh['expert'=16,'mp'=8,'batch'=2] {'expert'}, dimensions={0} | all-to-all | bytes 1105920 | tf_op jit(solution)/shard_map/all_to_all | solution.py:208
  204.1 1.1 copy.51
  205.3 3.4 copy.60
  208.6 4.6 %slice_bitcast_fusion.1 = (bf16[2880,360]{0,1:T(8,128)(2,1)}, bf16[2880,360]{0,1:T(8,128)(2,1)}) fusion(bf16[1,2,2880,360]{2,3,1,0:T(8,128)(2,1)} %param.22), kind=kLoop, calls=%fused_computation.20 | loop fusion | bytes 8294400 | tf_op jit(solution)/shard_map/squeeze | solution.py:215
  213.2 44.4 %all-gather.4.cloned.1.call-done = bf16[768,2880]{0,1:T(8,128)(2,1)} async-done(((bf16[768,360]{0,1:T(8,128)(2,1)}), bf16[768,2880]{0,1:T(8,128)(2,1)}) %all-gather.4.cloned.1.call-update) | async-done | bytes 4423696 | tf_op jit(solution)/shard_map/all_gather | solution.py:210
  257.6 3.3 fusion
  261.2 1.4 fusion.2
  263.5 3.6 fusion.5
  267.5 4.5 %convert_bitcast_fusion = bf16[8,768,360]{1,2,0:T(8,128)(2,1)} fusion(bf16[360,8,360]{0,2,1:T(8,128)(2,1)S(1)} %bitcast.140, bf16[768,360]{0,1:T(8,128)(2,1)S(1)} %fusion.28), kind=kOutput, calls=%fused_computation.12 | convolution fusion | flops 1594736640 | bytes 7050240 | tf_op jit(solution)/shard_map/rh,hjf->jrf/dot_general | solution.py:225
  272.0 57.1 %reduce-scatter.2.cloned.1.call-done = bf16[1,768,360]{1,2,0:T(8,128)(2,1)} async-done(((bf16[8,768,360]{1,2,0:T(8,128)(2,1)}), bf16[1,768,360]{1,2,0:T(8,128)(2,1)}) %reduce-scatter.2.cloned.1.call-update) | async-done | bytes 552976 | tf_op jit(solution)/shard_map/reduce_scatter | solution.py:231
  329.0 2.1 copy.53
  331.1 9.0 %all-to-all-start.5 = ((bf16[16,48,360]{2,1,0:T(8,128)(2,1)}), bf16[16,48,360]{2,1,0:T(8,128)(2,1)S(1)}, u32[]{:S(2)}, u32[]{:S(2)}) async-start(bf16[16,48,360]{2,1,0:T(8,128)(2,1)} %bitcast.40), calls=%async_computation.6 | async-start | bytes 1179648 | tf_op jit(solution)/shard_map/all_to_all | solution.py:235
  340.9 1.4 slice_bitcast_fusion.3
  342.3 15.2 %all-to-all-done.5 = bf16[16,48,360]{2,1,0:T(8,128)(2,1)S(1)} async-done(((bf16[16,48,360]{2,1,0:T(8,128)(2,1)}), bf16[16,48,360]{2,1,0:T(8,128)(2,1)S(1)}, u32[]{:S(2)}, u32[]{:S(2)}) %all-to-all-start.5) | async-done | bytes 552992 | tf_op jit(solution)/shard_map/all_to_all | solution.py:235
  (104 shorter events, 17.3 us)
Async XLA Ops:
  7.2 35.4 %copy-start.11 = (f32[2880]{0:T(1024)S(1)}, f32[2880]{0:T(1024)}, u32[]{:S(2)}) copy-start(f32[2880]{0:T(1024)} %param.15) | copy-start | bytes 34564
  7.2 136.4 %all-gather.6.cloned.1.call-start = ((), (), s32[]{:S(2)}) async-start(), calls=%async_computation.9 | async-start | bytes 6406144 | tf_op jit(solution)/shard_map/all_gather | solution.py:83
  10.9 18.3 %all-to-all-start = ((bf16[8,360,128]{2,1,0:T(8,128)(2,1)}), bf16[8,360,128]{2,1,0:T(8,128)(2,1)S(1)}, u32[]{:S(2)}, u32[]{:S(2)}) async-start(bf16[8,360,128]{2,1,0:T(8,128)(2,1)} %broadcast_in_dim.29), calls=%async_computation | async-start | bytes 1474560 | tf_op jit(solution)/shard_map/all_to_all | solution.py:42
  17.6 25.0 %copy-start.3 = (s32[1,128,4]{2,1,0:T(8,128)}, s32[1,128,4]{2,1,0:T(8,128)S(1)}, u32[]{:S(2)}) copy-start(s32[1,128,4]{2,1,0:T(8,128)S(1)} %copy.45) | copy-start | bytes 6148
  20.4 55.1 %copy-start.6 = (s32[16,4,128]{2,0,1:T(8,128)}, s32[16,4,128]{2,0,1:T(8,128)S(1)}, u32[]{:S(2)}) copy-start(s32[16,4,128]{2,0,1:T(8,128)S(1)} %reduce-window.6) | copy-start | bytes 98308
  30.2 38.9 %all-to-all-start.1 = ((bf16[16,180,128]{2,1,0:T(8,128)(2,1)}), bf16[16,180,128]{2,1,0:T(8,128)(2,1)S(1)}, u32[]{:S(2)}, u32[]{:S(2)}) async-start(bf16[16,180,128]{2,1,0:T(8,128)(2,1)} %broadcast_in_dim.30), calls=%async_computation.1 | async-start | bytes 1507328 | tf_op jit(solution)/shard_map/all_to_all | solution.py:42
  69.7 6.8 %copy-start.8 = (f32[128,128]{0,1:T(8,128)}, f32[128,128]{0,1:T(8,128)S(1)}, u32[]{:S(2)}) copy-start(f32[128,128]{0,1:T(8,128)S(1)} %fusion.68) | copy-start | bytes 196612
  70.9 82.7 %all-to-all-start.2 = ((bf16[16,128,128]{2,1,0:T(8,128)(2,1)}), bf16[16,128,128]{2,1,0:T(8,128)(2,1)S(1)}, u32[]{:S(2)}, u32[]{:S(2)}) async-start(bf16[16,128,128]{2,1,0:T(8,128)(2,1)} %broadcast_in_dim.35), calls=%async_computation.2 | async-start | bytes 1048576 | tf_op jit(solution)/shard_map/all_to_all | solution.py:42
  75.8 71.5 %copy-start.13 = (s32[16,5]{0,1:T(8,128)}, s32[16,5]{0,1:T(8,128)S(1)}, u32[]{:S(2)}) copy-start(s32[16,5]{0,1:T(8,128)S(1)} %reduce-window.9) | copy-start | bytes 964
  153.7 3.7 %copy-start.16 = (f32[8]{0:T(128)S(1)}, f32[8]{0:T(128)}, u32[]{:S(2)}) copy-start(f32[8]{0:T(128)} %param.20) | copy-start | bytes 100
  153.7 3.8 %copy-start.9 = (s32[1024]{0:T(1024)S(1)}, s32[1024]{0:T(1024)}, u32[]{:S(2)}) copy-start(s32[1024]{0:T(1024)} %get-tuple-element.61) | copy-start | bytes 12292
  153.7 3.8 %copy-start.10 = (s32[1024]{0:T(1024)S(1)}, s32[1024]{0:T(1024)}, u32[]{:S(2)}) copy-start(s32[1024]{0:T(1024)} %get-tuple-element.62) | copy-start | bytes 12292
  153.7 3.8 %copy-start.15 = (s32[1,2048]{1,0:T(1,128)S(1)}, s32[1,2048]{1,0:T(1,128)}, u32[]{:S(2)}) copy-start(s32[1,2048]{1,0:T(1,128)} %param.14) | copy-start | bytes 24580
  157.5 5.2 %slice-start = ((s8[6029312]{0:T(1024)(128)(4,1)}), s8[4194304]{0:T(1024)(128)(4,1)S(1)}, s32[]{:S(2)}) async-start(s8[6029312]{0:T(1024)(128)(4,1)} %bitcast.144), calls=%async_computation.10 | async-start | bytes 8388608
  157.5 5.2 %slice-start.1 = ((s8[6029312]{0:T(1024)(128)(4,1)}), s8[1835008]{0:T(1024)(128)(4,1)S(1)}, s32[]{:S(2)}) async-start(s8[6029312]{0:T(1024)(128)(4,1)} %bitcast.144), calls=%async_computation.11 | async-start | bytes 3670016
  162.6 6.1 %copy-start.4 = (s32[1,128,4]{2,1,0:T(8,128)S(1)}, s32[1,128,4]{2,1,0:T(8,128)}, u32[]{:S(2)}) copy-start(s32[1,128,4]{2,1,0:T(8,128)} %copy-done.3) | copy-start | bytes 6148
  162.6 6.2 %copy-start.7 = (s32[16,4,128]{2,0,1:T(8,128)S(1)}, s32[16,4,128]{2,0,1:T(8,128)}, u32[]{:S(2)}) copy-start(s32[16,4,128]{2,0,1:T(8,128)} %copy-done.6) | copy-start | bytes 98308
  162.7 6.2 %slice-start.2 = ((s32[16,5]{0,1:T(8,128)}), s32[16,4]{0,1:T(4,128)S(1)}, s32[]{:S(2)}) async-start(s32[16,5]{0,1:T(8,128)} %copy-done.13), calls=%async_computation.12 | async-start | bytes 4096 | tf_op jit(solution)/shard_map/slice.1
  162.7 6.2 %copy-start.14 = (s32[512]{0:T(512)S(1)}, s32[512]{0:T(512)}, u32[]{:S(2)}) copy-start(s32[512]{0:T(512)} %eq.110) | copy-start | bytes 6148
  162.7 18.5 %copy-start.5 = (bf16[1,128,360]{1,2,0:T(8,128)(2,1)S(1)}, bf16[1,128,360]{1,2,0:T(8,128)(2,1)}, u32[]{:S(2)}) copy-start(bf16[1,128,360]{1,2,0:T(8,128)(2,1)} %param.13) | copy-start | bytes 276484
  164.7 16.4 %all-to-all-start.3 = ((bf16[8,360,128]{2,1,0:T(8,128)(2,1)}), bf16[8,360,128]{2,1,0:T(8,128)(2,1)S(1)}, u32[]{:S(2)}, u32[]{:S(2)}) async-start(bf16[8,360,128]{2,1,0:T(8,128)(2,1)} %reshape.428), calls=%async_computation.3 | async-start | bytes 1474560 | tf_op jit(solution)/shard_map/all_to_all | solution.py:181
  168.7 88.9 %all-gather.4.cloned.1.call-start = ((), (), s32[]{:S(2)}) async-start(), calls=%async_computation.7 | async-start | bytes 4976640 | tf_op jit(solution)/shard_map/all_gather | solution.py:210
  205.2 123.8 %reduce-scatter.2.cloned.1.call-start = ((), (), s32[]{:S(2)}) async-start(), calls=%async_computation.8 | async-start | bytes 4976640 | tf_op jit(solution)/shard_map/reduce_scatter | solution.py:231
  213.2 47.8 %copy-start.12 = (f32[2880]{0:T(1024)S(1)}, f32[2880]{0:T(1024)}, u32[]{:S(2)}) copy-start(f32[2880]{0:T(1024)} %param.21) | copy-start | bytes 34564
  257.6 3.6 copy-start
  261.2 1.6 copy-start.1
  261.2 2.2 copy-start.2
  271.9 85.5 %copy-start.17 = (f32[1,128,4]{1,2,0:T(4,128)S(1)}, f32[1,128,4]{1,2,0:T(4,128)}, u32[]{:S(2)}) copy-start(f32[1,128,4]{1,2,0:T(4,128)} %param.25) | copy-start | bytes 6148
  331.1 26.4 %all-to-all-start.5 = ((bf16[16,48,360]{2,1,0:T(8,128)(2,1)}), bf16[16,48,360]{2,1,0:T(8,128)(2,1)S(1)}, u32[]{:S(2)}, u32[]{:S(2)}) async-start(bf16[16,48,360]{2,1,0:T(8,128)(2,1)} %bitcast.40), calls=%async_computation.6 | async-start | bytes 1179648 | tf_op jit(solution)/shard_map/all_to_all | solution.py:235
Sparse Core Ops, SparseCore 0:
  10.6 132.9 all-gather.5
  205.3 52.2 all-gather.3
  272.1 56.8 reduce-scatter.1
where the time goes:
time: 366 us; the launch traced here: 365 us
  waiting for transfers between devices  227 us (62%)
  starting transfers between devices  34.2 us (9%)
  local copies, waits for them, and re-layouts  33.1 us (9%)
  blocking collectives  22 us (6%)
  matrix products  17.8 us (5%)
  other arithmetic  16.8 us (5%)
  between operations  14.2 us (4%)
    all_gather x1, waiting for transfers between devices, shards(): lax.all_gather(jnp.pad(jnp.concatenate([w_query, w_out.T], axis=1), ((0,...  66 us
    reduce_scatter x1, waiting for transfers between devices, shards(): lax.psum_scatter(partials.astype(jnp.bfloat16), 'mp', scatter_dimension=0...  57.1 us
    all_gather x1, waiting for transfers between devices, shards(): lax.all_gather(arrived_rows, 'mp', axis=1, tiled=True)  44.4 us
    all_to_all x3, waiting for transfers between devices, gather_by_exchange(): lax.all_to_all(spread, axis_name, split_axis=0, concat_axis=0, tiled=True)  34.9 us
    all_to_all x1, blocking collectives, shards(): lax.all_to_all(outgoing, 'expert', split_axis=0, concat_axis=0, tiled=True)  22 us
    all_to_all x3, starting transfers between devices, gather_by_exchange(): lax.all_to_all(spread, axis_name, split_axis=0, concat_axis=0, tiled=True)  21.1 us
    all_to_all x1, waiting for transfers between devices, shards(): lax.all_to_all(expert_out, 'expert', split_axis=0, concat_axis=0, tiled=T...  15.2 us
    all_to_all x1, waiting for transfers between devices, shards(): lax.all_to_all(out_pieces, 'mp', split_axis=0, concat_axis=0, tiled=True)  9.69 us
  transfers between devices with their start and end apart: 8, of which 7 were waited for; matrix products, arithmetic and copies ran while one was open for 10% of the time, Pallas kernels for 0%

commit v1 on v0

--- a/solution.py
+++ b/solution.py
@@ -69,6 +69,13 @@
     routes,
     route_weights,
 ):
+
+    def _hold_strips_all(vec, shard_axis, d0):
+        small = lax.axis_size(shard_axis)
+        u_next = jnp.stack([vec] * small)
+        a_now = lax.all_to_all(u_next, axis_name=shard_axis, split_axis=0, concat_axis=0)
+        return jnp.concatenate(a_now, axis=d0)
+
     local_rows = tokens[0]
     tok_count = local_rows.shape[0]
     expert_devs = lax.axis_size("expert")
@@ -207,7 +214,7 @@
     )
     arrived = lax.all_to_all(outgoing, "expert", split_axis=0, concat_axis=0, tiled=True)
     arrived_rows = arrived.reshape(expert_count * capacity, arrived.shape[2])
-    inputs = rms_norm(lax.all_gather(arrived_rows, "mp", axis=1, tiled=True), moe_gain)
+    inputs = rms_norm(_hold_strips_all(arrived_rows, "mp", 1), moe_gain)
     w_in = expert_in[0]
     hidden_cols = w_in.shape[2]
     inputs = lax.optimization_barrier(inputs)

time: 366 us -> 385 us (1.052)
  waiting for transfers between devices: 227 us -> 239 us
  starting transfers between devices: 34.2 us -> 38.4 us
    all_gather x1 -> x0, waiting for transfers between devices: 44.4 us -> none  [shards(): lax.all_gather(arrived_rows, 'mp', axis=1, tiled=True)]
    all_to_all x0 -> x1, waiting for transfers between devices: none -> 44 us  [_hold_strips_all(): lax.all_to_all(u_next, axis_name=shard_axis, split_axis=0, concat_axis=0)]
    reduce_scatter x1, waiting for transfers between devices: 57.1 us -> 68.9 us  [shards(): lax.psum_scatter(partials.astype(jnp.bfloat16), 'mp', scatter_dimension=0...]
    all_to_all x0 -> x1, starting transfers between devices: none -> 4.57 us  [_hold_strips_all(): lax.all_to_all(u_next, axis_name=shard_axis, split_axis=0, concat_axis=0)]
  transfers between devices with their start and end apart: 8 -> 8, of which waited for: 7 -> 7; matrix products, arithmetic and copies ran while one was open for 10% -> 9% of each run, Pallas kernels for 0% -> 0%
where the time goes in v1:
time: 385 us; the launch traced here: 384 us
  waiting for transfers between devices  239 us (62%)
  starting transfers between devices  38.4 us (10%)
  local copies, waits for them, and re-layouts  34.1 us (9%)
  blocking collectives  21.8 us (6%)
  other arithmetic  18.4 us (5%)
  matrix products  17.8 us (5%)
  between operations  14.6 us (4%)
    reduce_scatter x1, waiting for transfers between devices, shards(): lax.psum_scatter(partials.astype(jnp.bfloat16), 'mp', scatter_dimension=0...  68.9 us
    all_gather x1, waiting for transfers between devices, shards(): lax.all_gather(jnp.pad(jnp.concatenate([w_query, w_out.T], axis=1), ((0,...  65.9 us
    all_to_all x1, waiting for transfers between devices, _hold_strips_all(): lax.all_to_all(u_next, axis_name=shard_axis, split_axis=0, concat_axis=0)  44 us
    all_to_all x3, waiting for transfers between devices, gather_by_exchange(): lax.all_to_all(spread, axis_name, split_axis=0, concat_axis=0, tiled=True)  35.3 us
    all_to_all x1, blocking collectives, shards(): lax.all_to_all(outgoing, 'expert', split_axis=0, concat_axis=0, tiled=True)  21.8 us
    all_to_all x3, starting transfers between devices, gather_by_exchange(): lax.all_to_all(spread, axis_name, split_axis=0, concat_axis=0, tiled=True)  20.6 us
    all_to_all x1, waiting for transfers between devices, shards(): lax.all_to_all(expert_out, 'expert', split_axis=0, concat_axis=0, tiled=T...  15.2 us
    all_to_all x1, waiting for transfers between devices, shards(): lax.all_to_all(out_pieces, 'mp', split_axis=0, concat_axis=0, tiled=True)  9.74 us
  transfers between devices with their start and end apart: 8, of which 7 were waited for; matrix products, arithmetic and copies ran while one was open for 9% of the time, Pallas kernels for 0%

profile of v1, /device:TPU:1, one launch (start us, length us, event | category | flops | bytes accessed | tf_op | source)
XLA Modules:
  0.0 384.2 jit_solution(4132506987101161328)
XLA Ops:
  7.2 1.8 fusion.36
  9.0 1.9 broadcast_in_dim.29
  10.9 5.9 %all-to-all-start = ((bf16[8,360,128]{2,1,0:T(8,128)(2,1)}), bf16[8,360,128]{2,1,0:T(8,128)(2,1)S(1)}, u32[]{:S(2)}, u32[]{:S(2)}) async-start(bf16[8,360,128]{2,1,0:T(8,128)(2,1)} %broadcast_in_dim.29), calls=%async_computation | async-start | bytes 1474560 | tf_op jit(solution)/shard_map/all_to_all | solution.py:42
  20.5 8.8 %all-to-all-done = bf16[8,360,128]{2,1,0:T(8,128)(2,1)S(1)} async-done(((bf16[8,360,128]{2,1,0:T(8,128)(2,1)}), bf16[8,360,128]{2,1,0:T(8,128)(2,1)S(1)}, u32[]{:S(2)}, u32[]{:S(2)}) %all-to-all-start) | async-done | bytes 737312 | tf_op jit(solution)/shard_map/all_to_all | solution.py:42
  30.2 10.6 %all-to-all-start.1 = ((bf16[16,180,128]{2,1,0:T(8,128)(2,1)}), bf16[16,180,128]{2,1,0:T(8,128)(2,1)S(1)}, u32[]{:S(2)}, u32[]{:S(2)}) async-start(bf16[16,180,128]{2,1,0:T(8,128)(2,1)} %broadcast_in_dim.30), calls=%async_computation.1 | async-start | bytes 1507328 | tf_op jit(solution)/shard_map/all_to_all | solution.py:42
  43.0 26.5 %all-to-all-done.1 = bf16[16,180,128]{2,1,0:T(8,128)(2,1)S(1)} async-done(((bf16[16,180,128]{2,1,0:T(8,128)(2,1)}), bf16[16,180,128]{2,1,0:T(8,128)(2,1)S(1)}, u32[]{:S(2)}, u32[]{:S(2)}) %all-to-all-start.1) | async-done | bytes 737312 | tf_op jit(solution)/shard_map/all_to_all | solution.py:42
  71.4 4.1 %all-to-all-start.2 = ((bf16[16,128,128]{2,1,0:T(8,128)(2,1)}), bf16[16,128,128]{2,1,0:T(8,128)(2,1)S(1)}, u32[]{:S(2)}, u32[]{:S(2)}) async-start(bf16[16,128,128]{2,1,0:T(8,128)(2,1)} %broadcast_in_dim.35), calls=%async_computation.2 | async-start | bytes 1048576 | tf_op jit(solution)/shard_map/all_to_all | solution.py:42
  77.6 65.9 %all-gather.3.cloned.1.call-done = bf16[2944,1024]{1,0:T(8,128)(2,1)} async-done(((bf16[184,1024]{1,0:T(8,128)(2,1)}), bf16[2944,1024]{1,0:T(8,128)(2,1)}) %all-gather.3.cloned.1.call-update) | async-done | bytes 6029328 | tf_op jit(solution)/shard_map/all_gather | solution.py:90
  143.5 3.8 slice.73
  147.3 3.3 copy.23
  150.7 2.1 fusion.66
  153.7 3.7 fusion.3
  157.5 3.5 convert_reduce_fusion
  161.1 1.5 fusion.23
  164.7 4.1 %all-to-all-start.3 = ((bf16[8,360,128]{2,1,0:T(8,128)(2,1)}), bf16[8,360,128]{2,1,0:T(8,128)(2,1)S(1)}, u32[]{:S(2)}, u32[]{:S(2)}) async-start(bf16[8,360,128]{2,1,0:T(8,128)(2,1)} %reshape.431), calls=%async_computation.3 | async-start | bytes 1474560 | tf_op jit(solution)/shard_map/all_to_all | solution.py:188
  169.1 2.4 scatter_custom_fusion
  171.6 9.7 %all-to-all-done.3 = bf16[8,360,128]{2,1,0:T(8,128)(2,1)S(1)} async-done(((bf16[8,360,128]{2,1,0:T(8,128)(2,1)}), bf16[8,360,128]{2,1,0:T(8,128)(2,1)S(1)}, u32[]{:S(2)}, u32[]{:S(2)}) %all-to-all-start.3) | async-done | bytes 737312 | tf_op jit(solution)/shard_map/all_to_all | solution.py:188
  182.2 21.8 %all_to_all.35 = bf16[16,48,360]{2,1,0:T(8,128)(2,1)S(1)} all-to-all(bf16[16,48,360]{2,1,0:T(8,128)(2,1)S(1)} %bitcast.146), channel_id=1, replica_groups=mesh['expert'=16,'mp'=8,'batch'=2] {'expert'}, dimensions={0} | all-to-all | bytes 1105920 | tf_op jit(solution)/shard_map/all_to_all | solution.py:215
  204.3 2.4 stack.3
  206.7 4.6 %all-to-all-start.5 = ((bf16[8,768,360]{1,2,0:T(8,128)(2,1)}), bf16[8,768,360]{1,2,0:T(8,128)(2,1)}, u32[]{:S(2)}, u32[]{:S(2)}) async-start(bf16[8,768,360]{1,2,0:T(8,128)(2,1)} %stack.3), calls=%async_computation.5 | async-start | bytes 8847360 | tf_op jit(solution)/shard_map/all_to_all | solution.py:76
  211.3 3.4 copy.45
  214.7 4.6 %slice_bitcast_fusion.1 = (bf16[2880,360]{0,1:T(8,128)(2,1)}, bf16[2880,360]{0,1:T(8,128)(2,1)}) fusion(bf16[1,2,2880,360]{2,3,1,0:T(8,128)(2,1)} %param.22), kind=kLoop, calls=%fused_computation.19 | loop fusion | bytes 8294400 | tf_op jit(solution)/shard_map/squeeze | solution.py:222
  219.3 44.0 %all-to-all-done.5 = bf16[8,768,360]{1,2,0:T(8,128)(2,1)} async-done(((bf16[8,768,360]{1,2,0:T(8,128)(2,1)}), bf16[8,768,360]{1,2,0:T(8,128)(2,1)}, u32[]{:S(2)}, u32[]{:S(2)}) %all-to-all-start.5) | async-done | bytes 4423712 | tf_op jit(solution)/shard_map/all_to_all | solution.py:76
  263.3 3.2 multiply_reduce_fusion
  266.5 3.2 fusion.1
  270.0 3.6 fusion.4
  274.0 4.5 %convert_bitcast_fusion = bf16[8,768,360]{1,2,0:T(8,128)(2,1)} fusion(bf16[360,8,360]{0,2,1:T(8,128)(2,1)S(1)} %bitcast.148, bf16[768,360]{0,1:T(8,128)(2,1)S(1)} %fusion.27), kind=kOutput, calls=%fused_computation.11 | convolution fusion | flops 1594736640 | bytes 7050240 | tf_op jit(solution)/shard_map/rh,hjf->jrf/dot_general | solution.py:232
  278.6 68.9 %reduce-scatter.2.cloned.1.call-done = bf16[1,768,360]{1,2,0:T(8,128)(2,1)} async-done(((bf16[8,768,360]{1,2,0:T(8,128)(2,1)}), bf16[1,768,360]{1,2,0:T(8,128)(2,1)}) %reduce-scatter.2.cloned.1.call-update) | async-done | bytes 552976 | tf_op jit(solution)/shard_map/reduce_scatter | solution.py:238
  347.6 2.1 copy.38
  349.7 9.0 %all-to-all-start.6 = ((bf16[16,48,360]{2,1,0:T(8,128)(2,1)}), bf16[16,48,360]{2,1,0:T(8,128)(2,1)S(1)}, u32[]{:S(2)}, u32[]{:S(2)}) async-start(bf16[16,48,360]{2,1,0:T(8,128)(2,1)} %bitcast.42), calls=%async_computation.7 | async-start | bytes 1179648 | tf_op jit(solution)/shard_map/all_to_all | solution.py:242
  359.5 1.4 slice_bitcast_fusion.3
  360.9 15.2 %all-to-all-done.6 = bf16[16,48,360]{2,1,0:T(8,128)(2,1)S(1)} async-done(((bf16[16,48,360]{2,1,0:T(8,128)(2,1)}), bf16[16,48,360]{2,1,0:T(8,128)(2,1)S(1)}, u32[]{:S(2)}, u32[]{:S(2)}) %all-to-all-start.6) | async-done | bytes 552992 | tf_op jit(solution)/shard_map/all_to_all | solution.py:242
  (102 shorter events, 18.1 us)
Async XLA Ops:
  7.2 35.4 %copy-start.10 = (f32[2880]{0:T(1024)S(1)}, f32[2880]{0:T(1024)}, u32[]{:S(2)}) copy-start(f32[2880]{0:T(1024)} %param.15) | copy-start | bytes 34564
  7.2 136.4 %all-gather.3.cloned.1.call-start = ((), (), s32[]{:S(2)}) async-start(), calls=%async_computation.9 | async-start | bytes 6406144 | tf_op jit(solution)/shard_map/all_gather | solution.py:90
  10.9 18.3 %all-to-all-start = ((bf16[8,360,128]{2,1,0:T(8,128)(2,1)}), bf16[8,360,128]{2,1,0:T(8,128)(2,1)S(1)}, u32[]{:S(2)}, u32[]{:S(2)}) async-start(bf16[8,360,128]{2,1,0:T(8,128)(2,1)} %broadcast_in_dim.29), calls=%async_computation | async-start | bytes 1474560 | tf_op jit(solution)/shard_map/all_to_all | solution.py:42
  17.6 25.0 %copy-start.2 = (s32[1,128,4]{2,1,0:T(8,128)}, s32[1,128,4]{2,1,0:T(8,128)S(1)}, u32[]{:S(2)}) copy-start(s32[1,128,4]{2,1,0:T(8,128)S(1)} %copy.30) | copy-start | bytes 6148
  20.4 55.1 %copy-start.5 = (s32[16,4,128]{2,0,1:T(8,128)}, s32[16,4,128]{2,0,1:T(8,128)S(1)}, u32[]{:S(2)}) copy-start(s32[16,4,128]{2,0,1:T(8,128)S(1)} %reduce-window.6) | copy-start | bytes 98308
  30.2 39.3 %all-to-all-start.1 = ((bf16[16,180,128]{2,1,0:T(8,128)(2,1)}), bf16[16,180,128]{2,1,0:T(8,128)(2,1)S(1)}, u32[]{:S(2)}, u32[]{:S(2)}) async-start(bf16[16,180,128]{2,1,0:T(8,128)(2,1)} %broadcast_in_dim.30), calls=%async_computation.1 | async-start | bytes 1507328 | tf_op jit(solution)/shard_map/all_to_all | solution.py:42
  70.1 6.4 %copy-start.7 = (f32[128,128]{0,1:T(8,128)}, f32[128,128]{0,1:T(8,128)S(1)}, u32[]{:S(2)}) copy-start(f32[128,128]{0,1:T(8,128)S(1)} %fusion.67) | copy-start | bytes 196612
  71.4 82.3 %all-to-all-start.2 = ((bf16[16,128,128]{2,1,0:T(8,128)(2,1)}), bf16[16,128,128]{2,1,0:T(8,128)(2,1)S(1)}, u32[]{:S(2)}, u32[]{:S(2)}) async-start(bf16[16,128,128]{2,1,0:T(8,128)(2,1)} %broadcast_in_dim.35), calls=%async_computation.2 | async-start | bytes 1048576 | tf_op jit(solution)/shard_map/all_to_all | solution.py:42
  75.8 71.6 %copy-start.12 = (s32[16,5]{0,1:T(8,128)}, s32[16,5]{0,1:T(8,128)S(1)}, u32[]{:S(2)}) copy-start(s32[16,5]{0,1:T(8,128)S(1)} %reduce-window.9) | copy-start | bytes 964
  153.7 3.7 copy-start.15
  153.7 3.8 copy-start.8
  153.7 3.8 copy-start.9
  153.7 3.8 copy-start.14
  157.5 5.2 %slice-start = ((s8[6029312]{0:T(1024)(128)(4,1)}), s8[4194304]{0:T(1024)(128)(4,1)S(1)}, s32[]{:S(2)}) async-start(s8[6029312]{0:T(1024)(128)(4,1)} %bitcast.152), calls=%async_computation.10 | async-start | bytes 8388608
  157.5 5.2 %slice-start.1 = ((s8[6029312]{0:T(1024)(128)(4,1)}), s8[1835008]{0:T(1024)(128)(4,1)S(1)}, s32[]{:S(2)}) async-start(s8[6029312]{0:T(1024)(128)(4,1)} %bitcast.152), calls=%async_computation.11 | async-start | bytes 3670016
  162.6 6.3 %copy-start.3 = (s32[1,128,4]{2,1,0:T(8,128)S(1)}, s32[1,128,4]{2,1,0:T(8,128)}, u32[]{:S(2)}) copy-start(s32[1,128,4]{2,1,0:T(8,128)} %copy-done.2) | copy-start | bytes 6148
  162.6 6.4 %copy-start.6 = (s32[16,4,128]{2,0,1:T(8,128)S(1)}, s32[16,4,128]{2,0,1:T(8,128)}, u32[]{:S(2)}) copy-start(s32[16,4,128]{2,0,1:T(8,128)} %copy-done.5) | copy-start | bytes 98308
  162.7 6.4 %slice-start.2 = ((s32[16,5]{0,1:T(8,128)}), s32[16,4]{0,1:T(4,128)S(1)}, s32[]{:S(2)}) async-start(s32[16,5]{0,1:T(8,128)} %copy-done.12), calls=%async_computation.12 | async-start | bytes 4096 | tf_op jit(solution)/shard_map/slice.1
  162.7 6.4 %copy-start.13 = (s32[512]{0:T(512)S(1)}, s32[512]{0:T(512)}, u32[]{:S(2)}) copy-start(s32[512]{0:T(512)} %eq.110) | copy-start | bytes 6148
  162.7 18.7 %copy-start.4 = (bf16[1,128,360]{1,2,0:T(8,128)(2,1)S(1)}, bf16[1,128,360]{1,2,0:T(8,128)(2,1)}, u32[]{:S(2)}) copy-start(bf16[1,128,360]{1,2,0:T(8,128)(2,1)} %param.13) | copy-start | bytes 276484
  164.7 16.6 %all-to-all-start.3 = ((bf16[8,360,128]{2,1,0:T(8,128)(2,1)}), bf16[8,360,128]{2,1,0:T(8,128)(2,1)S(1)}, u32[]{:S(2)}, u32[]{:S(2)}) async-start(bf16[8,360,128]{2,1,0:T(8,128)(2,1)} %reshape.431), calls=%async_computation.3 | async-start | bytes 1474560 | tf_op jit(solution)/shard_map/all_to_all | solution.py:188
  206.7 56.6 %all-to-all-start.5 = ((bf16[8,768,360]{1,2,0:T(8,128)(2,1)}), bf16[8,768,360]{1,2,0:T(8,128)(2,1)}, u32[]{:S(2)}, u32[]{:S(2)}) async-start(bf16[8,768,360]{1,2,0:T(8,128)(2,1)} %stack.3), calls=%async_computation.5 | async-start | bytes 8847360 | tf_op jit(solution)/shard_map/all_to_all | solution.py:76
  211.3 136.3 %reduce-scatter.2.cloned.1.call-start = ((), (), s32[]{:S(2)}) async-start(), calls=%async_computation.8 | async-start | bytes 4976640 | tf_op jit(solution)/shard_map/reduce_scatter | solution.py:238
  219.3 47.2 %copy-start.11 = (f32[2880]{0:T(1024)S(1)}, f32[2880]{0:T(1024)}, u32[]{:S(2)}) copy-start(f32[2880]{0:T(1024)} %param.21) | copy-start | bytes 34564
  266.5 3.2 copy-start
  266.5 3.6 copy-start.1
  278.6 97.5 %copy-start.16 = (f32[1,128,4]{1,2,0:T(4,128)S(1)}, f32[1,128,4]{1,2,0:T(4,128)}, u32[]{:S(2)}) copy-start(f32[1,128,4]{1,2,0:T(4,128)} %param.25) | copy-start | bytes 6148
  349.7 26.4 %all-to-all-start.6 = ((bf16[16,48,360]{2,1,0:T(8,128)(2,1)}), bf16[16,48,360]{2,1,0:T(8,128)(2,1)S(1)}, u32[]{:S(2)}, u32[]{:S(2)}) async-start(bf16[16,48,360]{2,1,0:T(8,128)(2,1)} %bitcast.42), calls=%async_computation.7 | async-start | bytes 1179648 | tf_op jit(solution)/shard_map/all_to_all | solution.py:242
Sparse Core Ops, SparseCore 0:
  10.6 132.8 all-gather.2
  278.7 68.7 reduce-scatter.1
